TPU v7x, 512 devices: a whole 4x8x8 slice. The times are simulated.
512 devices in a mesh: seq: 64 (over y, x, z_hi), head: 8 (over z_lo, core).
Axes of the slice: x: 4, y: 8, z: 8 (z_hi: 2, z_lo: 4; z = z_hi * 4 + z_lo), core: 2. Of those that a mesh axis runs over, the one named last changes fastest.
Arguments:
- queries: bfloat16 [32768, 16, 128], P('seq', 'head'), may hold values from -6 to 6
- keys: bfloat16 [32768, 16, 128], P('seq', 'head'), may hold values from -6 to 6
- values: bfloat16 [32768, 16, 128], P('seq', 'head'), may hold values from -6 to 6
- clusters: int32 [16, 32768, 1], P('head', 'seq'), may hold values from 0 to 255; in each aligned block of 512 rows (0 to 511, 512 to 1023, ..., all dimensions but the last counted through in order) at most 8 rows name the same one
- cent_keys: bfloat16 [16, 256, 128], P('head', 'seq'), may hold values from -6 to 6
- cent_values: bfloat16 [16, 256, 128], P('head', 'seq'), may hold values from -6 to 6
- out_weight: bfloat16 [2048, 4096], P('head'), may hold values from -0.1875 to 0.1875
Outputs:
- mixed: bfloat16 [4096, 32768], P('head', 'seq')
Inputs may be any that keep to these rules, and one draw needn't show every extreme that they name: `clusters`: among the 512 tokens of one device in one head (an aligned block of rows), no cluster is named more than 8 times; in some such block a cluster is named exactly 8 times.
All inputs are finite; a program needn't handle non-finite values.
Results may differ from a plain program's by a relative error of at most 0.017.
Values may be sent and summed in bfloat16 or wider, within the bound.
No kernel may reach another device: no remote copies, remote signals or barrier semaphores. Data moves between devices by JAX's collectives and lax.ppermute only.
A program may use at most 128 MiB of HBM per device.

v0:
```python
import jax
import jax.numpy as jnp
from jax import lax
from jax.sharding import PartitionSpec as P

CLUSTERS = 256
MOST = 8


def masked_scores(query_in, key_in, where_in, scale):
    sources, count, depth, width = query_in.shape
    nheads = where_in.shape[3]
    hsize = width // nheads
    query_five = query_in.reshape(sources, count, depth, nheads, hsize)
    key_five = key_in.reshape(sources, count, depth, nheads, hsize)
    raw = jnp.einsum(
        "aimhe,bikhe->ihambk", query_five, key_five, preferred_element_type=jnp.float32
    )
    scores = raw.reshape(count, nheads, sources * depth, sources * depth) * scale
    where_now = jnp.transpose(where_in, (1, 3, 0, 2)).reshape(count, nheads, sources * depth)
    allowed = (where_now[:, :, None, :] >= 0) & (
        where_now[:, :, None, :] <= where_now[:, :, :, None]
    )
    return (jnp.where(allowed, scores, -1e30), query_five)


def weigh_values(rounded, value_in):
    sources, count, depth, width = value_in.shape
    nheads = rounded.shape[1]
    value_five = value_in.reshape(sources, count, depth, nheads, width // nheads)
    shaped = rounded.reshape(count, nheads, sources * depth, sources, depth)
    return jnp.einsum("ihqbk,bikhe->ihqe", shaped, value_five, preferred_element_type=jnp.float32)


def to_slots(array_in, sources, depth):
    count, nheads = (array_in.shape[0], array_in.shape[1])
    tail = array_in.shape[3:]
    shaped = array_in.reshape((count, nheads, sources, depth) + tail)
    if len(tail) == 1:
        moved = jnp.transpose(shaped, (2, 0, 3, 1, 4))
        return moved.reshape(sources, count, depth, nheads * tail[0])
    return jnp.transpose(shaped, (2, 0, 3, 1))


def on_device(queries, keys, values, clusters, cent_keys, cent_values, out_weight):
    tok_dev, heads_dev, head_dim = queries.shape
    owners = lax.axis_size("seq")
    per_owner = CLUSTERS // owners
    slot_total = CLUSTERS * MOST
    scale = head_dim ** (-0.5)
    assign = clusters[:, :, 0]
    order = jnp.arange(tok_dev, dtype=jnp.int32)
    earlier = (assign[:, :, None] == assign[:, None, :]) & (
        order[None, None, :] < order[None, :, None]
    )
    rank = jnp.sum(earlier.astype(jnp.int32), axis=2)
    slot_of = (assign * MOST + rank).T
    head_cols = jnp.arange(heads_dev, dtype=jnp.int32)[None, :]
    position = lax.axis_index("seq") * tok_dev + order

    def place(rows_in):
        empty = jnp.zeros((slot_total, heads_dev, head_dim), rows_in.dtype)
        filled = empty.at[slot_of, head_cols].set(rows_in)
        return filled.reshape(owners, per_owner, MOST, heads_dev * head_dim)

    where_buf = jnp.full((slot_total, heads_dev), -1, jnp.int32)
    where_buf = where_buf.at[slot_of, head_cols].set(
        jnp.broadcast_to(position[:, None], (tok_dev, heads_dev))
    )
    where_buf = where_buf.reshape(owners, per_owner, MOST, heads_dev)
    cent_all_k, cent_all_v = (
        lax.all_gather(cent_keys, "seq", axis=1, tiled=True),
        lax.all_gather(cent_values, "seq", axis=1, tiled=True),
    )
    query_in = lax.all_to_all(place(queries), "seq", split_axis=0, concat_axis=0, tiled=True)
    key_in = lax.all_to_all(place(keys), "seq", split_axis=0, concat_axis=0, tiled=True)
    value_in = lax.all_to_all(place(values), "seq", split_axis=0, concat_axis=0, tiled=True)
    where_in = lax.all_to_all(where_buf, "seq", split_axis=0, concat_axis=0, tiled=True)
    sources, count, depth, width = query_in.shape
    local, query_five = masked_scores(query_in, key_in, where_in, scale)
    top = jnp.max(local, axis=-1, keepdims=True)
    w_local = jnp.exp(local - top)
    numer = weigh_values(w_local.astype(jnp.bfloat16), value_in)
    denom = jnp.sum(w_local, axis=-1)
    returned = (
        lax.all_to_all(
            to_slots(numer, sources, depth).astype(jnp.bfloat16),
            "seq",
            split_axis=0,
            concat_axis=0,
            tiled=True,
        ).astype(jnp.float32),
        lax.all_to_all(
            to_slots(top[..., 0], sources, depth).astype(jnp.bfloat16),
            "seq",
            split_axis=0,
            concat_axis=0,
            tiled=True,
        ).astype(jnp.float32),
        lax.all_to_all(
            to_slots(denom, sources, depth).astype(jnp.bfloat16),
            "seq",
            split_axis=0,
            concat_axis=0,
            tiled=True,
        ).astype(jnp.float32),
    )
    numer_s, top_s, denom_s = returned
    numer_t = numer_s.reshape(slot_total, heads_dev, head_dim)[slot_of, head_cols]
    top_t = top_s.reshape(slot_total, heads_dev)[slot_of, head_cols]
    denom_t = denom_s.reshape(slot_total, heads_dev)[slot_of, head_cols]
    memory = (
        jnp.einsum("the,hce->thc", queries, cent_all_k, preferred_element_type=jnp.float32) * scale
    )
    top = jnp.maximum(top_t, jnp.max(memory, axis=-1))
    w_memory = jnp.exp(memory - top[:, :, None])
    factor = jnp.exp(top_t - top)
    numer = numer_t * factor[:, :, None] + jnp.einsum(
        "thc,hce->the",
        w_memory.astype(jnp.bfloat16),
        cent_all_v,
        preferred_element_type=jnp.float32,
    )
    denom = denom_t * factor + jnp.sum(w_memory, axis=-1)
    attended = (numer / denom[:, :, None]).astype(jnp.bfloat16)
    flat_out = attended.reshape(tok_dev, heads_dev * head_dim)
    return lax.psum_scatter(
        jnp.einsum("kc,tk->ct", out_weight, flat_out, preferred_element_type=jnp.float32).astype(
            jnp.bfloat16
        ),
        "head",
        scatter_dimension=0,
        tiled=True,
    )


def solution(mesh):
    return jax.shard_map(
        on_device,
        mesh=mesh,
        in_specs=(
            P("seq", "head", None),
            P("seq", "head", None),
            P("seq", "head", None),
            P("head", "seq", None),
            P("head", "seq", None),
            P("head", "seq", None),
            P("head", None),
        ),
        out_specs=P("head", "seq"),
        check_vma=False,
    )
```

profile of v0, /device:TPU:2, one launch (start us, length us, event | category | flops | bytes accessed | tf_op | source)
XLA Modules:
  0.0 806.8 jit_solution(5865518857260931860)
XLA Ops:
  6.6 0.8 copy.192
  7.4 0.7 convert_reduce_fusion
  8.2 0.7 shift-left_or_fusion
  8.9 0.7 and_reduce_fusion
  9.6 0.8 multiply_reduce_fusion.1
  11.0 4.3 scatter_custom_fusion
  15.4 0.4 reshape.128
  15.7 0.7 copy.124
  16.5 19.1 %all-to-all-start = ((s32[64,4,8,2]{2,1,3,0:T(4,128)}), s32[64,4,8,2]{2,1,3,0:T(4,128)S(1)}, u32[]{:S(2)}, u32[]{:S(2)}) async-start(s32[64,4,8,2]{2,1,3,0:T(4,128)} %copy.124), calls=%async_computation | async-start | bytes 524288 | tf_op jit(solution)/shard_map/all_to_all | solution.py:78
  35.9 3.9 scatter_custom_fusion.1
  39.8 1.2 reshape.129
  41.0 10.4 %all-to-all-done = s32[64,4,8,2]{2,1,3,0:T(4,128)S(1)} async-done(((s32[64,4,8,2]{2,1,3,0:T(4,128)}), s32[64,4,8,2]{2,1,3,0:T(4,128)S(1)}, u32[]{:S(2)}, u32[]{:S(2)}) %all-to-all-start) | async-done | bytes 16416 | tf_op jit(solution)/shard_map/all_to_all | solution.py:78
  51.5 6.4 all-to-all-start.1
  57.9 3.9 scatter_custom_fusion.2
  61.8 1.2 reshape.131
  63.0 25.8 %all-to-all-done.1 = bf16[64,4,8,256]{3,2,1,0:T(8,128)(2,1)} async-done(((bf16[64,4,8,256]{3,2,1,0:T(8,128)(2,1)}), bf16[64,4,8,256]{3,2,1,0:T(8,128)(2,1)}, u32[]{:S(2)}, u32[]{:S(2)}) %all-to-all-start.1) | async-done | bytes 1048608 | tf_op jit(solution)/shard_map/all_to_all | solution.py:75
  88.8 7.1 all-to-all-start.2
  95.9 4.1 scatter_custom_fusion.3
  99.9 1.2 reshape.133
  101.5 24.8 %all-to-all-done.2 = bf16[64,4,8,256]{3,2,1,0:T(8,128)(2,1)} async-done(((bf16[64,4,8,256]{3,2,1,0:T(8,128)(2,1)}), bf16[64,4,8,256]{3,2,1,0:T(8,128)(2,1)}, u32[]{:S(2)}, u32[]{:S(2)}) %all-to-all-start.2) | async-done | bytes 1048608 | tf_op jit(solution)/shard_map/all_to_all | solution.py:76
  126.3 7.2 all-to-all-start.3
  133.5 6.9 fusion
  140.4 5.7 copy-done.1
  146.1 6.4 exponential_reduce_fusion
  152.8 9.4 %copy.130 = f32[4,2,64,8,64,8]{4,5,3,2,1,0:T(8,128)S(1)} copy(f32[4,2,64,8,64,8]{4,3,5,2,1,0:T(8,128)} %copy-done.1) | data formatting | bytes 16777216 | tf_op jit(solution)/shard_map/mul | solution.py:19
  162.2 0.8 copy.148
  162.9 12.5 %exponential_convert_fusion = bf16[4,2,512,64,8]{3,4,2,1,0:T(8,128)(2,1)} fusion(f32[4,2,512,64,8]{3,4,2,1,0:T(8,128)S(1)} %bitcast.84, f32[4,2,512]{2,1,0:T(2,128)S(1)} %sub.34, s32[4,2,512]{2,1,0:T(2,128)S(1)} %le.25, s32[4,2,64,8]{2,3,1,0:T(8,128)S(1)} %bitcast.91, pred[4,2,64,8]{2,3,1,0:T(8,128)(4,1)S(1)} %broadcast_compare_fusion), kind=kLoop, calls=%fused_computation.8 | loop fusion | flops 10485760 | bytes 12636160 | tf_op jit(solution)/shard_map/convert_element_type | solution.py:83
  175.4 15.1 %all-to-all-start.6 = ((bf16[64,4,8,2]{2,1,3,0:T(4,128)(2,1)}), bf16[64,4,8,2]{2,1,3,0:T(4,128)(2,1)S(1)}, u32[]{:S(2)}, u32[]{:S(2)}) async-start(bf16[64,4,8,2]{2,1,3,0:T(4,128)(2,1)} %copy.148), calls=%async_computation.6 | async-start | bytes 262144 | tf_op jit(solution)/shard_map/all_to_all | solution.py:100
  190.6 0.8 copy.136
  191.3 12.0 %copy.132 = bf16[4,2,512,64,8]{2,4,3,1,0:T(8,128)(2,1)} copy(bf16[4,2,512,64,8]{3,4,2,1,0:T(8,128)(2,1)} %exponential_convert_fusion) | data formatting | bytes 8388608 | tf_op jit(solution)/shard_map/convert_element_type | solution.py:83
  203.3 1.2 all-to-all-done.6
  204.5 13.9 %all-to-all-start.5 = ((bf16[64,4,8,2]{2,1,3,0:T(4,128)(2,1)}), bf16[64,4,8,2]{2,1,3,0:T(4,128)(2,1)S(1)}, u32[]{:S(2)}, u32[]{:S(2)}) async-start(bf16[64,4,8,2]{2,1,3,0:T(4,128)(2,1)} %copy.136), calls=%async_computation.5 | async-start | bytes 262144 | tf_op jit(solution)/shard_map/all_to_all | solution.py:93
  218.5 4.0 fusion.2
  222.5 1.3 copy.190
  223.8 8.5 %all-to-all-done.5 = bf16[64,4,8,2]{2,1,3,0:T(4,128)(2,1)S(1)} async-done(((bf16[64,4,8,2]{2,1,3,0:T(4,128)(2,1)}), bf16[64,4,8,2]{2,1,3,0:T(4,128)(2,1)S(1)}, u32[]{:S(2)}, u32[]{:S(2)}) %all-to-all-start.5) | async-done | bytes 8224 | tf_op jit(solution)/shard_map/all_to_all | solution.py:93
  232.3 6.8 all-to-all-start.4
  239.5 224.9 %all_gather.6 = bf16[2,256,128]{2,0,1:T(2,128)(2,1)S(1)} all-gather(bf16[2,4,128]{2,0,1:T(2,128)(2,1)S(1)} %copy.139), channel_id=1, replica_groups=mesh['seq'=64,'head'=8] {'seq'}, dimensions={1}, use_global_device_ids=true | all-gather | bytes 133120 | tf_op jit(solution)/shard_map/all_gather | solution.py:72
  464.4 227.6 %all_gather.7 = bf16[2,256,128]{2,0,1:T(2,128)(2,1)} all-gather(bf16[2,4,128]{2,0,1:T(2,128)(2,1)S(1)} %copy.145), channel_id=1, replica_groups=mesh['seq'=64,'head'=8] {'seq'}, dimensions={1}, use_global_device_ids=true | all-gather | bytes 133120 | tf_op jit(solution)/shard_map/all_gather | solution.py:73
  692.0 1.9 fusion.27
  694.5 9.1 %gather_fusion.2 = f32[1024]{0:T(1024)S(1)} fusion(f32[2048,2]{0,1:T(2,128)S(1)} %reshape.166, s32[1024]{0:T(1024)S(1)} %reshape.167), kind=kCustom, calls=%fused_computation.2 | custom fusion | bytes 16384 | tf_op jit(solution)/shard_map/gather | solution.py:111
  704.4 9.1 %gather_fusion.1 = f32[1024]{0:T(1024)S(1)} fusion(f32[2048,2]{0,1:T(2,128)S(1)} %reshape.164, s32[1024]{0:T(1024)S(1)} %reshape.167), kind=kCustom, calls=%fused_computation.1 | custom fusion | bytes 16384 | tf_op jit(solution)/shard_map/gather | solution.py:110
  714.1 3.1 reshape.162
  717.2 16.2 %gather_fusion = f32[1024,128]{1,0:T(8,128)} fusion(f32[2048,2,128]{2,1,0:T(2,128)} %reshape.162, s32[1024]{0:T(1024)S(1)} %reshape.167), kind=kCustom, calls=%fused_computation | custom fusion | bytes 1056768 | tf_op jit(solution)/shard_map/gather | solution.py:109
  733.4 2.0 copy.144
  735.4 1.4 fusion.6
  736.9 3.2 fusion.1
  740.1 57.8 %reduce-scatter.2.cloned.1.call-done = bf16[512,512]{0,1:T(8,128)(2,1)} async-done(((bf16[4096,512]{0,1:T(8,128)(2,1)}), bf16[512,512]{0,1:T(8,128)(2,1)}) %reduce-scatter.2.cloned.1.call-update) | async-done | bytes 524304 | tf_op jit(solution)/shard_map/reduce_scatter | solution.py:127
  797.9 2.0 copy.152
  (51 shorter events, 3.8 us)
Async XLA Ops:
  6.5 730.3 %copy-start = (bf16[256,4096]{1,0:T(8,128)(2,1)S(1)}, bf16[256,4096]{1,0:T(8,128)(2,1)}, u32[]{:S(2)}) copy-start(bf16[256,4096]{1,0:T(8,128)(2,1)} %param.13) | copy-start | bytes 6291460
  16.5 35.0 %all-to-all-start = ((s32[64,4,8,2]{2,1,3,0:T(4,128)}), s32[64,4,8,2]{2,1,3,0:T(4,128)S(1)}, u32[]{:S(2)}, u32[]{:S(2)}) async-start(s32[64,4,8,2]{2,1,3,0:T(4,128)} %copy.124), calls=%async_computation | async-start | bytes 524288 | tf_op jit(solution)/shard_map/all_to_all | solution.py:78
  51.5 37.3 %all-to-all-start.1 = ((bf16[64,4,8,256]{3,2,1,0:T(8,128)(2,1)}), bf16[64,4,8,256]{3,2,1,0:T(8,128)(2,1)}, u32[]{:S(2)}, u32[]{:S(2)}) async-start(bf16[64,4,8,256]{3,2,1,0:T(8,128)(2,1)} %reshape.129), calls=%async_computation.1 | async-start | bytes 2097152 | tf_op jit(solution)/shard_map/all_to_all | solution.py:75
  88.8 37.5 %all-to-all-start.2 = ((bf16[64,4,8,256]{3,2,1,0:T(8,128)(2,1)}), bf16[64,4,8,256]{3,2,1,0:T(8,128)(2,1)}, u32[]{:S(2)}, u32[]{:S(2)}) async-start(bf16[64,4,8,256]{3,2,1,0:T(8,128)(2,1)} %reshape.131), calls=%async_computation.2 | async-start | bytes 2097152 | tf_op jit(solution)/shard_map/all_to_all | solution.py:76
  126.3 49.1 %all-to-all-start.3 = ((bf16[64,4,8,256]{3,2,1,0:T(8,128)(2,1)}), bf16[64,4,8,256]{3,2,1,0:T(8,128)(2,1)}, u32[]{:S(2)}, u32[]{:S(2)}) async-start(bf16[64,4,8,256]{3,2,1,0:T(8,128)(2,1)} %reshape.133), calls=%async_computation.3 | async-start | bytes 2097152 | tf_op jit(solution)/shard_map/all_to_all | solution.py:77
  140.4 5.7 copy-start.1
  175.4 29.1 %all-to-all-start.6 = ((bf16[64,4,8,2]{2,1,3,0:T(4,128)(2,1)}), bf16[64,4,8,2]{2,1,3,0:T(4,128)(2,1)S(1)}, u32[]{:S(2)}, u32[]{:S(2)}) async-start(bf16[64,4,8,2]{2,1,3,0:T(4,128)(2,1)} %copy.148), calls=%async_computation.6 | async-start | bytes 262144 | tf_op jit(solution)/shard_map/all_to_all | solution.py:100
  204.5 27.8 %all-to-all-start.5 = ((bf16[64,4,8,2]{2,1,3,0:T(4,128)(2,1)}), bf16[64,4,8,2]{2,1,3,0:T(4,128)(2,1)S(1)}, u32[]{:S(2)}, u32[]{:S(2)}) async-start(bf16[64,4,8,2]{2,1,3,0:T(4,128)(2,1)} %copy.136), calls=%async_computation.5 | async-start | bytes 262144 | tf_op jit(solution)/shard_map/all_to_all | solution.py:93
  218.5 21.0 %copy-start.5 = (bf16[2,4,128]{2,1,0:T(4,128)(2,1)S(1)}, bf16[2,4,128]{2,1,0:T(4,128)(2,1)}, u32[]{:S(2)}) copy-start(bf16[2,4,128]{2,1,0:T(4,128)(2,1)} %param.11) | copy-start | bytes 6148
  218.5 21.0 %copy-start.6 = (bf16[2,4,128]{2,1,0:T(4,128)(2,1)S(1)}, bf16[2,4,128]{2,1,0:T(4,128)(2,1)}, u32[]{:S(2)}) copy-start(bf16[2,4,128]{2,1,0:T(4,128)(2,1)} %param.12) | copy-start | bytes 6148
  218.5 473.5 %copy-start.3 = (bf16[512,2,128]{2,1,0:T(2,128)(2,1)S(1)}, bf16[512,2,128]{2,1,0:T(2,128)(2,1)}, u32[]{:S(2)}) copy-start(bf16[512,2,128]{2,1,0:T(2,128)(2,1)} %param.7) | copy-start | bytes 786436
  232.3 481.8 %all-to-all-start.4 = ((bf16[64,4,8,256]{3,2,1,0:T(8,128)(2,1)}), bf16[64,4,8,256]{3,2,1,0:T(8,128)(2,1)}, u32[]{:S(2)}, u32[]{:S(2)}) async-start(bf16[64,4,8,256]{3,2,1,0:T(8,128)(2,1)} %bitcast.81), calls=%async_computation.4 | async-start | bytes 2097152 | tf_op jit(solution)/shard_map/all_to_all | solution.py:86
  239.1 558.8 %reduce-scatter.2.cloned.1.call-start = ((), (), s32[]{:S(2)}) async-start(), calls=%async_computation.8 | async-start | bytes 4718592 | tf_op jit(solution)/shard_map/reduce_scatter | solution.py:127
  704.4 9.4 %copy-start.4 = (f32[512,2]{0,1:T(2,128)S(1)}, f32[512,2]{0,1:T(2,128)}, u32[]{:S(2)}) copy-start(f32[512,2]{0,1:T(2,128)} %get-tuple-element.15) | copy-start | bytes 12292
  704.4 9.4 %copy-start.2 = (f32[512,2,256]{0,2,1:T(8,128)S(1)}, f32[512,2,256]{0,2,1:T(8,128)}, u32[]{:S(2)}) copy-start(f32[512,2,256]{0,2,1:T(8,128)} %get-tuple-element.16) | copy-start | bytes 3145732
Sparse Core Ops, SparseCore 0:
  740.3 57.6 reduce-scatter.1
where the time goes:
time: 808 us; the launch traced here: 807 us
  blocking collectives  453 us (56%)
  waiting for transfers between devices  129 us (16%)
  local copies, waits for them, and re-layouts  96.7 us (12%)
  starting transfers between devices  75.7 us (9%)
  other arithmetic  22.2 us (3%)
  matrix products  17.4 us (2%)
  between operations  13.8 us (2%)
    all_gather x1, blocking collectives, on_device(): lax.all_gather(cent_values, 'seq', axis=1, tiled=True)  228 us
    all_gather x1, blocking collectives, on_device(): lax.all_gather(cent_keys, 'seq', axis=1, tiled=True)  225 us
    reduce_scatter x1, waiting for transfers between devices, on_device(): lax.psum_scatter(jnp.einsum('kc,tk->ct', out_weight, flat_out, preferred_...  57.8 us
    all_to_all x1, waiting for transfers between devices, on_device(): lax.all_to_all(place(queries), 'seq', split_axis=0, concat_axis=0, tiled=...  25.8 us
    all_to_all x1, waiting for transfers between devices, on_device(): lax.all_to_all(place(keys), 'seq', split_axis=0, concat_axis=0, tiled=True)  24.8 us
    unnamed x26, local copies, waits for them, and re-layouts  23.4 us
    all_to_all x1, starting transfers between devices, on_device(): lax.all_to_all(where_buf, 'seq', split_axis=0, concat_axis=0, tiled=True)  19.1 us
    gather x2, local copies, waits for them, and re-layouts, on_device(): numer_s.reshape(slot_total, heads_dev, head_dim)[slot_of, head_cols]  18.3 us
  transfers between devices with their start and end apart: 8, of which 6 were waited for; matrix products, arithmetic and copies ran while one was open for 11% of the time, Pallas kernels for 0%

commit v1 on v0

--- a/solution.py
+++ b/solution.py
@@ -68,8 +68,14 @@
         jnp.broadcast_to(position[:, None], (tok_dev, heads_dev))
     )
     where_buf = where_buf.reshape(owners, per_owner, MOST, heads_dev)
+    guide_spot = lambda piece_in: jnp.concatenate(
+        lax.all_to_all(
+            jnp.stack([piece_in for _ in range(lax.axis_size("seq"))], axis=0), "seq", 0, 0
+        ),
+        axis=1,
+    )
     cent_all_k, cent_all_v = (
-        lax.all_gather(cent_keys, "seq", axis=1, tiled=True),
+        guide_spot(cent_keys),
         lax.all_gather(cent_values, "seq", axis=1, tiled=True),
     )
     query_in = lax.all_to_all(place(queries), "seq", split_axis=0, concat_axis=0, tiled=True)

time: 808 us -> 612 us (0.76)
  blocking collectives: 453 us -> 234 us
  starting transfers between devices: 75.7 us -> 90.2 us
    all_gather x1 -> x0, blocking collectives: 225 us -> none  [on_device(): lax.all_gather(cent_keys, 'seq', axis=1, tiled=True)]
    unnamed x26 -> x23, local copies, waits for them, and re-layouts: 23.4 us -> 17.7 us
  transfers between devices with their start and end apart: 8 -> 9, of which waited for: 6 -> 7; matrix products, arithmetic and copies ran while one was open for 11% -> 17% of each run, Pallas kernels for 0% -> 0%
where the time goes in v1:
time: 612 us; the launch traced here: 610 us
  blocking collectives  234 us (38%)
  waiting for transfers between devices  132 us (22%)
  local copies, waits for them, and re-layouts  91.7 us (15%)
  starting transfers between devices  90.2 us (15%)
  other arithmetic  25 us (4%)
  matrix products  23.9 us (4%)
  between operations  13.8 us (2%)
    all_gather x1, blocking collectives, on_device(): lax.all_gather(cent_values, 'seq', axis=1, tiled=True)  234 us
    reduce_scatter x1, waiting for transfers between devices, on_device(): lax.psum_scatter(jnp.einsum('kc,tk->ct', out_weight, flat_out, preferred_...  60.3 us
    all_to_all x1, waiting for transfers between devices, on_device(): lax.all_to_all(place(queries), 'seq', split_axis=0, concat_axis=0, tiled=...  25.8 us
    all_to_all x1, waiting for transfers between devices, on_device(): lax.all_to_all(place(keys), 'seq', split_axis=0, concat_axis=0, tiled=True)  24.8 us
    all_to_all x1, starting transfers between devices, on_device(): lax.all_to_all(where_buf, 'seq', split_axis=0, concat_axis=0, tiled=True)  19.1 us
    gather x2, local copies, waits for them, and re-layouts, on_device(): numer_s.reshape(slot_total, heads_dev, head_dim)[slot_of, head_cols]  18.3 us
    unnamed x23, local copies, waits for them, and re-layouts  17.7 us
    all_to_all x1, starting transfers between devices, on_device(): lax.all_to_all(to_slots(denom, sources, depth).astype(jnp.bfloat16), 'seq...  15.1 us
  transfers between devices with their start and end apart: 9, of which 7 were waited for; matrix products, arithmetic and copies ran while one was open for 17% of the time, Pallas kernels for 0%

profile of v1, /device:TPU:2, one launch (start us, length us, event | category | flops | bytes accessed | tf_op | source)
XLA Modules:
  0.0 610.2 jit_solution(8008699133833834012)
XLA Ops:
  6.6 0.8 copy.185
  7.4 0.7 convert_reduce_fusion
  8.2 0.7 shift-left_or_fusion
  8.9 0.7 and_reduce_fusion
  9.6 0.8 multiply_reduce_fusion.1
  11.0 4.3 scatter_custom_fusion
  15.8 0.7 copy.122
  16.5 19.1 %all-to-all-start = ((s32[64,4,8,2]{2,1,3,0:T(4,128)}), s32[64,4,8,2]{2,1,3,0:T(4,128)S(1)}, u32[]{:S(2)}, u32[]{:S(2)}) async-start(s32[64,4,8,2]{2,1,3,0:T(4,128)} %copy.122), calls=%async_computation | async-start | bytes 524288 | tf_op jit(solution)/shard_map/all_to_all | solution.py:84
  35.9 3.9 scatter_custom_fusion.1
  39.8 1.2 reshape.137
  41.1 10.4 %all-to-all-done = s32[64,4,8,2]{2,1,3,0:T(4,128)S(1)} async-done(((s32[64,4,8,2]{2,1,3,0:T(4,128)}), s32[64,4,8,2]{2,1,3,0:T(4,128)S(1)}, u32[]{:S(2)}, u32[]{:S(2)}) %all-to-all-start) | async-done | bytes 16416 | tf_op jit(solution)/shard_map/all_to_all | solution.py:84
  51.5 6.4 %all-to-all-start.1 = ((bf16[64,4,8,256]{3,2,1,0:T(8,128)(2,1)}), bf16[64,4,8,256]{3,2,1,0:T(8,128)(2,1)}, u32[]{:S(2)}, u32[]{:S(2)}) async-start(bf16[64,4,8,256]{3,2,1,0:T(8,128)(2,1)} %reshape.137), calls=%async_computation.1 | async-start | bytes 2097152 | tf_op jit(solution)/shard_map/all_to_all | solution.py:81
  57.9 3.9 scatter_custom_fusion.2
  61.8 1.2 reshape.139
  63.0 25.8 %all-to-all-done.1 = bf16[64,4,8,256]{3,2,1,0:T(8,128)(2,1)} async-done(((bf16[64,4,8,256]{3,2,1,0:T(8,128)(2,1)}), bf16[64,4,8,256]{3,2,1,0:T(8,128)(2,1)}, u32[]{:S(2)}, u32[]{:S(2)}) %all-to-all-start.1) | async-done | bytes 1048608 | tf_op jit(solution)/shard_map/all_to_all | solution.py:81
  88.8 7.1 %all-to-all-start.2 = ((bf16[64,4,8,256]{3,2,1,0:T(8,128)(2,1)}), bf16[64,4,8,256]{3,2,1,0:T(8,128)(2,1)}, u32[]{:S(2)}, u32[]{:S(2)}) async-start(bf16[64,4,8,256]{3,2,1,0:T(8,128)(2,1)} %reshape.139), calls=%async_computation.2 | async-start | bytes 2097152 | tf_op jit(solution)/shard_map/all_to_all | solution.py:82
  95.9 4.1 scatter_custom_fusion.3
  100.0 1.2 reshape.141
  101.5 24.8 %all-to-all-done.2 = bf16[64,4,8,256]{3,2,1,0:T(8,128)(2,1)} async-done(((bf16[64,4,8,256]{3,2,1,0:T(8,128)(2,1)}), bf16[64,4,8,256]{3,2,1,0:T(8,128)(2,1)}, u32[]{:S(2)}, u32[]{:S(2)}) %all-to-all-start.2) | async-done | bytes 1048608 | tf_op jit(solution)/shard_map/all_to_all | solution.py:82
  126.3 0.7 stack.2
  127.0 7.0 %all-to-all-start.6 = ((bf16[64,2,4,128]{3,2,1,0:T(4,128)(2,1)}), bf16[64,2,4,128]{3,2,1,0:T(4,128)(2,1)S(1)}, u32[]{:S(2)}, u32[]{:S(2)}) async-start(bf16[64,2,4,128]{3,2,1,0:T(4,128)(2,1)} %stack.2), calls=%async_computation.6 | async-start | bytes 262144 | tf_op jit(solution)/shard_map/all_to_all | solution.py:72
  134.1 13.3 %fusion = (f32[4,2,64,8]{3,2,1,0:T(8,128)S(1)}, f32[4,2,64,8,64,8]{4,3,5,2,1,0:T(8,128)}) fusion(s32[4,2,64,8]{3,2,1,0:T(8,128)S(1)} %bitcast.89, s32[4,2,64,8]{2,3,1,0:T(8,128)S(1)} %bitcast.92, pred[4,2,64,8]{2,3,1,0:T(8,128)(4,1)S(1)} %broadcast_compare_fusion, bf16[64,4,8,2,128,1]{4,2,3,1,0,5:T(8,128)(2,1)} %bitcast.10, ...), kind=kOutput, calls=%fused_computation.10 | convolution fusion | flops 547352576 | bytes 10539008 | tf_op jit(solution)/shard_map/aimhe,bikhe->ihambk/dot_general | solution.py:16
  147.4 0.6 all-to-all-done.6
  148.0 14.7 %all-to-all-start.3 = ((bf16[64,4,8,256]{3,2,1,0:T(8,128)(2,1)}), bf16[64,4,8,256]{3,2,1,0:T(8,128)(2,1)}, u32[]{:S(2)}, u32[]{:S(2)}) async-start(bf16[64,4,8,256]{3,2,1,0:T(8,128)(2,1)} %reshape.141), calls=%async_computation.3 | async-start | bytes 2097152 | tf_op jit(solution)/shard_map/all_to_all | solution.py:83
  162.7 9.2 %exponential_reduce_fusion = bf16[4,2,64,8]{3,2,1,0:T(8,128)(2,1)S(1)} fusion(f32[4,2,64,8,64,8]{4,3,5,2,1,0:T(8,128)} %get-tuple-element.14, f32[4,2,64,8]{3,2,1,0:T(8,128)S(1)} %get-tuple-element.13, s32[4,2,64,8]{3,2,1,0:T(8,128)S(1)} %bitcast.90, s32[4,2,64,8]{2,3,1,0:T(8,128)S(1)} %bitcast.93, pred[4,2,64,8]{2,3,1,0:T(8,128)(4,1)S(1)} %broadcast_compare_fusion), kind=kLoop, calls=%fused_computation.7 | loop fusion | flops 10481664 | bytes 8450048 | tf_op jit(solution)/shard_map/reduce_sum | solution.py:90
  172.1 9.4 %copy.128 = f32[4,2,64,8,64,8]{4,5,3,2,1,0:T(8,128)S(1)} copy(f32[4,2,64,8,64,8]{4,3,5,2,1,0:T(8,128)} %get-tuple-element.14) | data formatting | bytes 16777216 | tf_op jit(solution)/shard_map/mul | solution.py:19
  181.5 0.8 copy.145
  182.3 12.5 %exponential_convert_fusion = bf16[4,2,512,64,8]{3,4,2,1,0:T(8,128)(2,1)} fusion(f32[4,2,512,64,8]{3,4,2,1,0:T(8,128)S(1)} %bitcast.87, f32[4,2,512]{2,1,0:T(2,128)S(1)} %sub.34, s32[4,2,512]{2,1,0:T(2,128)S(1)} %le.25, s32[4,2,64,8]{2,3,1,0:T(8,128)S(1)} %bitcast.94, pred[4,2,64,8]{2,3,1,0:T(8,128)(4,1)S(1)} %broadcast_compare_fusion), kind=kLoop, calls=%fused_computation.8 | loop fusion | flops 10485760 | bytes 12636160 | tf_op jit(solution)/shard_map/convert_element_type | solution.py:89
  194.8 15.1 %all-to-all-start.7 = ((bf16[64,4,8,2]{2,1,3,0:T(4,128)(2,1)}), bf16[64,4,8,2]{2,1,3,0:T(4,128)(2,1)S(1)}, u32[]{:S(2)}, u32[]{:S(2)}) async-start(bf16[64,4,8,2]{2,1,3,0:T(4,128)(2,1)} %copy.145), calls=%async_computation.7 | async-start | bytes 262144 | tf_op jit(solution)/shard_map/all_to_all | solution.py:106
  209.9 0.8 copy.134
  210.7 12.0 %copy.130 = bf16[4,2,512,64,8]{2,4,3,1,0:T(8,128)(2,1)} copy(bf16[4,2,512,64,8]{3,4,2,1,0:T(8,128)(2,1)} %exponential_convert_fusion) | data formatting | bytes 8388608 | tf_op jit(solution)/shard_map/convert_element_type | solution.py:89
  222.7 1.0 all-to-all-done.7
  223.7 14.1 %all-to-all-start.5 = ((bf16[64,4,8,2]{2,1,3,0:T(4,128)(2,1)}), bf16[64,4,8,2]{2,1,3,0:T(4,128)(2,1)S(1)}, u32[]{:S(2)}, u32[]{:S(2)}) async-start(bf16[64,4,8,2]{2,1,3,0:T(4,128)(2,1)} %copy.134), calls=%async_computation.5 | async-start | bytes 262144 | tf_op jit(solution)/shard_map/all_to_all | solution.py:99
  237.8 4.0 fusion.2
  241.8 1.3 copy.183
  243.1 8.6 %all-to-all-done.5 = bf16[64,4,8,2]{2,1,3,0:T(4,128)(2,1)S(1)} async-done(((bf16[64,4,8,2]{2,1,3,0:T(4,128)(2,1)}), bf16[64,4,8,2]{2,1,3,0:T(4,128)(2,1)S(1)}, u32[]{:S(2)}, u32[]{:S(2)}) %all-to-all-start.5) | async-done | bytes 8224 | tf_op jit(solution)/shard_map/all_to_all | solution.py:99
  251.7 6.7 %all-to-all-start.4 = ((bf16[64,4,8,256]{3,2,1,0:T(8,128)(2,1)}), bf16[64,4,8,256]{3,2,1,0:T(8,128)(2,1)}, u32[]{:S(2)}, u32[]{:S(2)}) async-start(bf16[64,4,8,256]{3,2,1,0:T(8,128)(2,1)} %bitcast.84), calls=%async_computation.4 | async-start | bytes 2097152 | tf_op jit(solution)/shard_map/all_to_all | solution.py:92
  258.8 234.0 %all_gather.3 = bf16[2,256,128]{2,0,1:T(2,128)(2,1)} all-gather(bf16[2,4,128]{2,0,1:T(2,128)(2,1)S(1)} %copy.142), channel_id=1, replica_groups=mesh['seq'=64,'head'=8] {'seq'}, dimensions={1}, use_global_device_ids=true | all-gather | bytes 133120 | tf_op jit(solution)/shard_map/all_gather | solution.py:79
  492.9 1.9 fusion.26
  495.3 9.1 %gather_fusion.2 = f32[1024]{0:T(1024)S(1)} fusion(f32[2048,2]{0,1:T(2,128)S(1)} %reshape.176, s32[1024]{0:T(1024)S(1)} %reshape.177), kind=kCustom, calls=%fused_computation.2 | custom fusion | bytes 16384 | tf_op jit(solution)/shard_map/gather | solution.py:117
  505.3 9.1 %gather_fusion.1 = f32[1024]{0:T(1024)S(1)} fusion(f32[2048,2]{0,1:T(2,128)S(1)} %reshape.174, s32[1024]{0:T(1024)S(1)} %reshape.177), kind=kCustom, calls=%fused_computation.1 | custom fusion | bytes 16384 | tf_op jit(solution)/shard_map/gather | solution.py:116
  514.9 3.1 reshape.172
  518.0 16.2 %gather_fusion = f32[1024,128]{1,0:T(8,128)} fusion(f32[2048,2,128]{2,1,0:T(2,128)} %reshape.172, s32[1024]{0:T(1024)S(1)} %reshape.177), kind=kCustom, calls=%fused_computation | custom fusion | bytes 1056768 | tf_op jit(solution)/shard_map/gather | solution.py:115
  534.2 2.0 copy.141
  536.3 1.4 fusion.6
  537.7 3.2 fusion.1
  541.0 60.3 %reduce-scatter.2.cloned.1.call-done = bf16[512,512]{0,1:T(8,128)(2,1)} async-done(((bf16[4096,512]{0,1:T(8,128)(2,1)}), bf16[512,512]{0,1:T(8,128)(2,1)}) %reduce-scatter.2.cloned.1.call-update) | async-done | bytes 524304 | tf_op jit(solution)/shard_map/reduce_scatter | solution.py:133
  601.3 2.0 copy.149
  (51 shorter events, 4.2 us)
Async XLA Ops:
  6.5 531.2 %copy-start = (bf16[256,4096]{1,0:T(8,128)(2,1)S(1)}, bf16[256,4096]{1,0:T(8,128)(2,1)}, u32[]{:S(2)}) copy-start(bf16[256,4096]{1,0:T(8,128)(2,1)} %param.13) | copy-start | bytes 6291460
  11.0 115.3 %copy-start.4 = (bf16[2,4,128]{2,1,0:T(4,128)(2,1)S(1)}, bf16[2,4,128]{2,1,0:T(4,128)(2,1)}, u32[]{:S(2)}) copy-start(bf16[2,4,128]{2,1,0:T(4,128)(2,1)} %param.11) | copy-start | bytes 6148
  16.5 35.0 %all-to-all-start = ((s32[64,4,8,2]{2,1,3,0:T(4,128)}), s32[64,4,8,2]{2,1,3,0:T(4,128)S(1)}, u32[]{:S(2)}, u32[]{:S(2)}) async-start(s32[64,4,8,2]{2,1,3,0:T(4,128)} %copy.122), calls=%async_computation | async-start | bytes 524288 | tf_op jit(solution)/shard_map/all_to_all | solution.py:84
  51.5 37.3 %all-to-all-start.1 = ((bf16[64,4,8,256]{3,2,1,0:T(8,128)(2,1)}), bf16[64,4,8,256]{3,2,1,0:T(8,128)(2,1)}, u32[]{:S(2)}, u32[]{:S(2)}) async-start(bf16[64,4,8,256]{3,2,1,0:T(8,128)(2,1)} %reshape.137), calls=%async_computation.1 | async-start | bytes 2097152 | tf_op jit(solution)/shard_map/all_to_all | solution.py:81
  88.8 37.6 %all-to-all-start.2 = ((bf16[64,4,8,256]{3,2,1,0:T(8,128)(2,1)}), bf16[64,4,8,256]{3,2,1,0:T(8,128)(2,1)}, u32[]{:S(2)}, u32[]{:S(2)}) async-start(bf16[64,4,8,256]{3,2,1,0:T(8,128)(2,1)} %reshape.139), calls=%async_computation.2 | async-start | bytes 2097152 | tf_op jit(solution)/shard_map/all_to_all | solution.py:82
  127.0 20.9 %all-to-all-start.6 = ((bf16[64,2,4,128]{3,2,1,0:T(4,128)(2,1)}), bf16[64,2,4,128]{3,2,1,0:T(4,128)(2,1)S(1)}, u32[]{:S(2)}, u32[]{:S(2)}) async-start(bf16[64,2,4,128]{3,2,1,0:T(4,128)(2,1)} %stack.2), calls=%async_computation.6 | async-start | bytes 262144 | tf_op jit(solution)/shard_map/all_to_all | solution.py:72
  148.0 46.8 %all-to-all-start.3 = ((bf16[64,4,8,256]{3,2,1,0:T(8,128)(2,1)}), bf16[64,4,8,256]{3,2,1,0:T(8,128)(2,1)}, u32[]{:S(2)}, u32[]{:S(2)}) async-start(bf16[64,4,8,256]{3,2,1,0:T(8,128)(2,1)} %reshape.141), calls=%async_computation.3 | async-start | bytes 2097152 | tf_op jit(solution)/shard_map/all_to_all | solution.py:83
  194.8 28.9 %all-to-all-start.7 = ((bf16[64,4,8,2]{2,1,3,0:T(4,128)(2,1)}), bf16[64,4,8,2]{2,1,3,0:T(4,128)(2,1)S(1)}, u32[]{:S(2)}, u32[]{:S(2)}) async-start(bf16[64,4,8,2]{2,1,3,0:T(4,128)(2,1)} %copy.145), calls=%async_computation.7 | async-start | bytes 262144 | tf_op jit(solution)/shard_map/all_to_all | solution.py:106
  223.7 28.0 %all-to-all-start.5 = ((bf16[64,4,8,2]{2,1,3,0:T(4,128)(2,1)}), bf16[64,4,8,2]{2,1,3,0:T(4,128)(2,1)S(1)}, u32[]{:S(2)}, u32[]{:S(2)}) async-start(bf16[64,4,8,2]{2,1,3,0:T(4,128)(2,1)} %copy.134), calls=%async_computation.5 | async-start | bytes 262144 | tf_op jit(solution)/shard_map/all_to_all | solution.py:99
  237.8 21.0 %copy-start.5 = (bf16[2,4,128]{2,1,0:T(4,128)(2,1)S(1)}, bf16[2,4,128]{2,1,0:T(4,128)(2,1)}, u32[]{:S(2)}) copy-start(bf16[2,4,128]{2,1,0:T(4,128)(2,1)} %param.12) | copy-start | bytes 6148
  237.8 255.0 %copy-start.2 = (bf16[512,2,128]{2,1,0:T(2,128)(2,1)S(1)}, bf16[512,2,128]{2,1,0:T(2,128)(2,1)}, u32[]{:S(2)}) copy-start(bf16[512,2,128]{2,1,0:T(2,128)(2,1)} %param.7) | copy-start | bytes 786436
  251.7 263.2 %all-to-all-start.4 = ((bf16[64,4,8,256]{3,2,1,0:T(8,128)(2,1)}), bf16[64,4,8,256]{3,2,1,0:T(8,128)(2,1)}, u32[]{:S(2)}, u32[]{:S(2)}) async-start(bf16[64,4,8,256]{3,2,1,0:T(8,128)(2,1)} %bitcast.84), calls=%async_computation.4 | async-start | bytes 2097152 | tf_op jit(solution)/shard_map/all_to_all | solution.py:92
  258.4 342.9 %reduce-scatter.2.cloned.1.call-start = ((), (), s32[]{:S(2)}) async-start(), calls=%async_computation.9 | async-start | bytes 4718592 | tf_op jit(solution)/shard_map/reduce_scatter | solution.py:133
  505.3 9.4 %copy-start.3 = (f32[512,2]{0,1:T(2,128)S(1)}, f32[512,2]{0,1:T(2,128)}, u32[]{:S(2)}) copy-start(f32[512,2]{0,1:T(2,128)} %get-tuple-element.15) | copy-start | bytes 12292
  505.3 9.4 %copy-start.1 = (f32[512,2,256]{0,2,1:T(8,128)S(1)}, f32[512,2,256]{0,2,1:T(8,128)}, u32[]{:S(2)}) copy-start(f32[512,2,256]{0,2,1:T(8,128)} %get-tuple-element.16) | copy-start | bytes 3145732
Sparse Core Ops, SparseCore 0:
  541.1 60.1 reduce-scatter.1
